TPU v7x, 256 devices: a whole 4x4x8 slice. The times are simulated.
256 devices in a mesh: probe: 16 (over z, x_lo), slab: 16 (over x_hi, y, core).
Axes of the slice: x: 4 (x_hi: 2, x_lo: 2; x = x_hi * 2 + x_lo), y: 4, z: 8, core: 2. Of those that a mesh axis runs over, the one named last changes fastest.
Arguments:
- u_prev: float32 [512, 128, 128], P('slab', 'probe'), may hold values from -6 to 6
- u_cur: float32 [512, 128, 128], P('slab', 'probe'), may hold values from -6 to 6
- buoyancy: float32 [512, 128, 128], P('slab'), may hold values from 0.6 to 1.4
- kappa: float32 [512, 128, 128], P('slab'), may hold values from 0.06 to 0.14
- dkappa: float32 [16, 512, 128, 128], P('probe', 'slab'), may hold values from -0.3 to 0.3
- du_prev: float32 [16, 512, 128, 128], P('probe', 'slab'), may hold values from -6 to 6
- du_cur: float32 [16, 512, 128, 128], P('probe', 'slab'), may hold values from -6 to 6
Outputs:
- background_first: float32 [512, 128, 128], P('slab', 'probe')
- background_second: float32 [512, 128, 128], P('slab', 'probe')
- born_first: float32 [16, 512, 128, 128], P('probe', 'slab')
- born_second: float32 [16, 512, 128, 128], P('probe', 'slab')
All inputs are finite; a program needn't handle non-finite values.
Results may differ from a plain program's by a relative error of at most 0.00002.
Values sent between devices are 32-bit elements; how exact they have to be, the bound alone decides.
No kernel may reach another device: no remote copies, remote signals or barrier semaphores. Data moves between devices by JAX's collectives and lax.ppermute only.
A program may use at most 128 MiB of HBM per device.

v0:
```python
import jax
import jax.numpy as jnp
from jax import lax
from jax.sharding import PartitionSpec as P

SECOND = (-205.0 / 72.0, 8.0 / 5.0, -1.0 / 5.0, 8.0 / 315.0, -1.0 / 560.0)
FIRST = (0.0, 4.0 / 5.0, -1.0 / 5.0, 4.0 / 105.0, -1.0 / 280.0)


def extended_2(cells, sides, width):
    for axis, dim in sides:
        count = lax.axis_size(axis)
        ends = count - 1
        head = lax.slice_in_dim(cells, 0, width, axis=dim)
        tail = lax.slice_in_dim(cells, cells.shape[dim] - width, cells.shape[dim], axis=dim)
        cells = jnp.concatenate(
            [
                lax.ppermute(tail, axis, [(i, (i + 1) % count) for i in range(ends)]),
                cells,
                lax.ppermute(head, axis, [((i + 1) % count, i) for i in range(ends)]),
            ],
            axis=dim,
        )
    return cells


def derivatives(extended):
    array_rank = extended.ndim
    center = extended[..., 4:-4, 4:-4, 4:-4]
    cores = (
        extended[..., :, 4:-4, 4:-4],
        extended[..., 4:-4, :, 4:-4],
        extended[..., 4:-4, 4:-4, :],
    )
    second = 3.0 * SECOND[0] * center
    gradients = []
    for dimension in range(3):
        source = cores[dimension]
        axis_place = array_rank - 3 + dimension
        extent = center.shape[axis_place]
        gradient = jnp.zeros_like(center)
        for distance in range(1, 5):
            higher = lax.slice_in_dim(source, 4 + distance, 4 + distance + extent, axis=axis_place)
            deeper = lax.slice_in_dim(source, 4 - distance, 4 - distance + extent, axis=axis_place)
            second = second + SECOND[distance] * (higher + deeper)
            gradient = gradient + FIRST[distance] * (higher - deeper)
        gradients.append(gradient)
    return (second, gradients[0], gradients[1], gradients[2])


def operate(extended, buoyancy, slopes):
    second, depth_slope, cross_slope, lateral_slope = derivatives(extended)
    return (
        buoyancy * second
        + slopes[0] * depth_slope
        + slopes[1] * cross_slope
        + slopes[2] * lateral_slope
    )


def local(u_prev, u_cur, buoyancy, kappa, dkappa, du_prev, du_cur):
    strip = u_cur.shape[1]
    offset = lax.axis_index("probe") * strip
    rimmed = extended_2(buoyancy, (("slab", 0),), 4)
    buoyancy_widths = [(0, 0), (4, 4), (4, 4)]
    unused, slope_one, slope_two, slope_three = derivatives(jnp.pad(rimmed, buoyancy_widths))
    slopes = (slope_one, slope_two, slope_three)
    probe_kappa = dkappa[0]
    older = du_prev[0]
    newer = du_cur[0]
    born_states = []
    background_states = []

    def cut_strip(field):
        return lax.dynamic_slice_in_dim(field, offset, strip, 1)

    strip_buoyancy = cut_strip(buoyancy)
    strip_kappa = cut_strip(kappa)
    strip_slopes = (cut_strip(slope_one), cut_strip(slope_two), cut_strip(slope_three))
    background_old = u_prev
    background_new = u_cur
    for repeat in range(2):
        extended = extended_2(background_new, (("probe", 1), ("slab", 0)), 4)
        extended = jnp.pad(extended, [(0, 0), (0, 0), (4, 4)])
        image_strip = operate(extended, strip_buoyancy, strip_slopes)
        background_next = 2.0 * background_new - background_old + strip_kappa * image_strip
        image_whole = lax.all_gather(image_strip, "probe", axis=1, tiled=True)
        born_rimmed = extended_2(newer, (("slab", 0),), 4)
        born_image = operate(jnp.pad(born_rimmed, [(0, 0), (4, 4), (4, 4)]), buoyancy, slopes)
        born_next = 2.0 * newer - older + kappa * born_image + probe_kappa * image_whole
        background_states.append(background_next)
        born_states.append(born_next)
        background_old, background_new = (background_new, background_next)
        older, newer = (newer, born_next)
    return (background_states[0], background_states[1], born_states[0][None], born_states[1][None])


def solution(mesh):
    return jax.shard_map(
        local,
        mesh=mesh,
        in_specs=(
            P("slab", "probe", None),
            P("slab", "probe", None),
            P("slab", None, None),
            P("slab", None, None),
            P("probe", "slab", None, None),
            P("probe", "slab", None, None),
            P("probe", "slab", None, None),
        ),
        out_specs=(
            P("slab", "probe", None),
            P("slab", "probe", None),
            P("probe", "slab", None, None),
            P("probe", "slab", None, None),
        ),
        check_vma=False,
    )
```

profile of v0, /device:TPU:6, one launch (start us, length us, event | category | flops | bytes accessed | tf_op | source)
XLA Modules:
  0.0 289.8 jit_solution(7251088802055237671)
XLA Ops:
  7.2 1.1 fusion.51
  8.3 5.2 %collective-permute-start.4 = (f32[4,128,128]{2,1,0:T(8,128)S(1)}, f32[4,128,128]{2,1,0:T(8,128)S(1)}, u32[]{:S(2)}, u32[]{:S(2)}) collective-permute-start(f32[4,128,128]{2,1,0:T(8,128)S(1)} %get-tuple-element.17), channel_id=1, source_target_pairs={{1,0},{2,1},{3,2},{4,3},{5,4},{6,5},{7,6},{8,7},{9,8},{10,9},{11,1... | collective-permute-start | bytes 786440 | tf_op jit(solution)/shard_map/ppermute | solution.py:20
  13.5 1.9 collective-permute-start.5
  15.5 1.0 fusion.53
  16.5 1.9 collective-permute-start.1
  18.4 4.8 %collective-permute-start = (f32[32,4,128]{2,1,0:T(4,128)S(1)}, f32[32,4,128]{2,1,0:T(4,128)S(1)}, u32[]{:S(2)}, u32[]{:S(2)}) collective-permute-start(f32[32,4,128]{2,1,0:T(4,128)S(1)} %get-tuple-element.28), channel_id=1, source_target_pairs={{0,16},{16,32},{32,48},{48,64},{64,80},{80,96},{96,112},{112,128},... | collective-permute-start | bytes 196616 | tf_op jit(solution)/shard_map/ppermute | solution.py:18
  23.2 1.1 constant_dynamic-update-slice_fusion.1
  24.3 0.8 collective-permute-done
  25.1 0.8 pad_maximum_fusion.12
  25.9 6.1 %collective-permute-start.2 = (f32[4,16,128]{2,1,0:T(8,128)S(1)}, f32[4,16,128]{2,1,0:T(8,128)S(1)}, u32[]{:S(2)}, u32[]{:S(2)}) collective-permute-start(f32[4,16,128]{2,1,0:T(8,128)S(1)} %get-tuple-element.25), channel_id=1, source_target_pairs={{1,0},{2,1},{3,2},{4,3},{5,4},{6,5},{7,6},{8,7},{9,8},{10,9},{11,1... | collective-permute-start | bytes 98312 | tf_op jit(solution)/shard_map/ppermute | solution.py:20
  32.0 1.9 collective-permute-start.3
  34.0 0.7 copy-done.6
  34.7 6.2 %collective-permute-done.3 = f32[4,16,128]{2,1,0:T(8,128)S(1)} collective-permute-done((f32[4,16,128]{2,1,0:T(8,128)S(1)}, f32[4,16,128]{2,1,0:T(8,128)S(1)}, u32[]{:S(2)}, u32[]{:S(2)}) %collective-permute-start.3) | collective-permute-done | bytes 32800 | tf_op jit(solution)/shard_map/ppermute | solution.py:18
  40.9 0.8 pad_maximum_fusion.4
  41.6 0.4 select_maximum_fusion.10
  42.0 0.7 copy-done.8
  42.7 4.6 %select_maximum_fusion.4 = f32[40,136,136]{2,1,0:T(8,128)S(1)} fusion(f32[4,128,128]{2,1,0:T(8,128)} %copy-done.8, f32[32,128,128]{2,1,0:T(8,128)S(1)} %copy-done, f32[4,128,128]{2,1,0:T(8,128)} %collective-permute-done.5), kind=kLoop, calls=%fused_computation.8 | loop fusion | flops 11097600 | bytes 5580800 | tf_op jit(solution)/shard_map/concatenate | solution.py:16
  47.3 9.8 %fusion.23 = (f32[32,128,128]{2,1,0:T(8,128)}, f32[32,128,128]{2,1,0:T(8,128)}) fusion(f32[40,136,136]{2,1,0:T(8,128)S(1)} %select_maximum_fusion.4), kind=kLoop, calls=%fused_computation.66 | loop fusion | flops 11534336 | bytes 37748736 | tf_op jit(solution)/shard_map/add | solution.py:46
  57.1 1.0 constant_dynamic-update-slice_fusion.5
  58.1 2.1 constant_dynamic-update-slice_fusion.3
  60.3 2.0 fusion.30
  62.3 1.4 copy-done.2
  63.7 2.3 multiply_add_fusion.2
  66.0 0.0 all-gather.5.cloned.1.call-start
  66.0 1.1 slice_bitcast_fusion
  67.1 1.9 collective-permute-start.10
  69.0 2.4 collective-permute-start.11
  71.5 1.9 collective-permute-start.7
  73.4 4.8 %collective-permute-start.6 = (f32[32,4,128]{2,1,0:T(4,128)S(1)}, f32[32,4,128]{2,1,0:T(4,128)S(1)}, u32[]{:S(2)}, u32[]{:S(2)}) collective-permute-start(f32[32,4,128]{2,1,0:T(4,128)S(1)} %get-tuple-element.26), channel_id=1, source_target_pairs={{0,16},{16,32},{32,48},{48,64},{64,80},{80,96},{96,112},{112,128},... | collective-permute-start | bytes 196616 | tf_op jit(solution)/shard_map/ppermute | solution.py:18
  78.2 0.4 collective-permute-done.7
  78.6 2.4 collective-permute-done.6
  81.0 5.2 %collective-permute-start.8 = (f32[4,16,128]{2,1,0:T(8,128)S(1)}, f32[4,16,128]{2,1,0:T(8,128)S(1)}, u32[]{:S(2)}, u32[]{:S(2)}) collective-permute-start(f32[4,16,128]{2,1,0:T(8,128)S(1)} %get-tuple-element.21), channel_id=1, source_target_pairs={{1,0},{2,1},{3,2},{4,3},{5,4},{6,5},{7,6},{8,7},{9,8},{10,9},{11,1... | collective-permute-start | bytes 98312 | tf_op jit(solution)/shard_map/ppermute | solution.py:20
  86.3 2.1 collective-permute-start.9
  88.4 6.5 %select_maximum_fusion.2 = f32[40,136,136]{2,1,0:T(8,128)} fusion(f32[4,128,128]{2,1,0:T(8,128)S(1)} %collective-permute-done.10, f32[32,128,128]{2,1,0:T(8,128)} %bitcast.24, f32[4,128,128]{2,1,0:T(8,128)S(1)} %collective-permute-done.11), kind=kLoop, calls=%fused_computation.6 | loop fusion | flops 11097600 | bytes 5580800 | tf_op jit(solution)/shard_map/concatenate | solution.py:16
  94.9 1.2 collective-permute-done.9
  96.1 0.1 pad_maximum_fusion.5
  96.2 0.4 select_maximum_fusion.6
  96.6 2.4 multiply_add_fusion
  99.0 53.2 %all-gather.3.cloned.1.call-done = f32[32,128,128]{2,1,0:T(8,128)} async-done(((f32[32,8,128]{2,1,0:T(8,128)}), f32[32,128,128]{2,1,0:T(8,128)}) %all-gather.3.cloned.1.call-update) | async-done | bytes 2097168 | tf_op jit(solution)/shard_map/all_gather | solution.py:87
  152.3 48.3 %fusion.36 = f32[32,128,128]{2,1,0:T(8,128)} fusion(f32[32,128,128]{2,1,0:T(8,128)} %all-gather.3.cloned.1.call-done, f32[1,32,128,128]{3,2,1,0:T(8,128)} %param.11, f32[1,32,128,128]{3,2,1,0:T(8,128)} %param.12, f32[32,128,128]{2,1,0:T(8,128)} %param.10, f32[32,128,128]{2,1,0:T(8,128)} %get-tuple-element.9, f32[32,128,128]{2,1,0:T(8,128)} %get-tuple-element.8, ...), kind=kLoop, calls=%fused_computation.88 | loop fusion | flops 47710208 | bytes 55050240 | tf_op jit(solution)/shard_map/add | solution.py:90
  200.6 1.1 fusion.50
  201.6 1.9 collective-permute-start.12
  203.6 2.6 collective-permute-start.13
  206.2 6.6 %collective-permute-done.12 = f32[4,128,128]{2,1,0:T(8,128)S(1)} collective-permute-done((f32[4,128,128]{2,1,0:T(8,128)S(1)}, f32[4,128,128]{2,1,0:T(8,128)S(1)}, u32[]{:S(2)}, u32[]{:S(2)}) %collective-permute-start.12) | collective-permute-done | bytes 262176 | tf_op jit(solution)/shard_map/ppermute | solution.py:20
  212.8 5.7 %collective-permute-done.13 = f32[4,128,128]{2,1,0:T(8,128)S(1)} collective-permute-done((f32[4,128,128]{2,1,0:T(8,128)S(1)}, f32[4,128,128]{2,1,0:T(8,128)S(1)}, u32[]{:S(2)}, u32[]{:S(2)}) %collective-permute-start.13) | collective-permute-done | bytes 262176 | tf_op jit(solution)/shard_map/ppermute | solution.py:18
  218.5 6.5 %select_maximum_fusion = f32[40,136,136]{2,1,0:T(8,128)} fusion(f32[4,128,128]{2,1,0:T(8,128)S(1)} %collective-permute-done.12, f32[32,128,128]{2,1,0:T(8,128)} %fusion.36, f32[4,128,128]{2,1,0:T(8,128)S(1)} %collective-permute-done.13), kind=kLoop, calls=%fused_computation.4 | loop fusion | flops 11097600 | bytes 5580800 | tf_op jit(solution)/shard_map/concatenate | solution.py:16
  225.0 8.6 %all-gather.5.cloned.1.call-done = f32[32,128,128]{2,1,0:T(8,128)} async-done(((f32[32,8,128]{2,1,0:T(8,128)}), f32[32,128,128]{2,1,0:T(8,128)}) %all-gather.5.cloned.1.call-update) | async-done | bytes 2097168 | tf_op jit(solution)/shard_map/all_gather | solution.py:87
  233.6 49.3 %fusion.38 = f32[1,32,128,128]{3,2,1,0:T(8,128)} fusion(f32[32,128,128]{2,1,0:T(8,128)} %all-gather.5.cloned.1.call-done, f32[1,32,128,128]{3,2,1,0:T(8,128)} %param.11, f32[32,128,128]{2,1,0:T(8,128)} %param.10, f32[32,128,128]{2,1,0:T(8,128)} %get-tuple-element.9, f32[32,128,128]{2,1,0:T(8,128)} %get-tuple-element.8, f32[32,128,128]{2,1,0:T(8,128)} %copy-done.2, ...), kind=kLoop, calls=%fused_computation.90 | loop fusion | flops 47710208 | bytes 55050240 | tf_op jit(solution)/shard_map/broadcast_in_dim | solution.py:95
  (33 shorter events, 0.2 us)
Async XLA Ops:
  7.2 33.7 %copy-start.3 = (f32[32,8,128]{2,1,0:T(8,128)S(1)}, f32[32,8,128]{2,1,0:T(8,128)}, u32[]{:S(2)}) copy-start(f32[32,8,128]{2,1,0:T(8,128)} %param.8) | copy-start | bytes 393220
  7.2 145.1 %all-gather.3.cloned.1.call-start = ((), (), s32[]{:S(2)}) async-start(), calls=%async_computation | async-start | bytes 2228224 | tf_op jit(solution)/shard_map/all_gather | solution.py:87
  8.3 33.7 %collective-permute-start.4 = (f32[4,128,128]{2,1,0:T(8,128)S(1)}, f32[4,128,128]{2,1,0:T(8,128)S(1)}, u32[]{:S(2)}, u32[]{:S(2)}) collective-permute-start(f32[4,128,128]{2,1,0:T(8,128)S(1)} %get-tuple-element.17), channel_id=1, source_target_pairs={{1,0},{2,1},{3,2},{4,3},{5,4},{6,5},{7,6},{8,7},{9,8},{10,9},{11,1... | collective-permute-start | bytes 786440 | tf_op jit(solution)/shard_map/ppermute | solution.py:20
  13.5 29.2 %collective-permute-start.5 = (f32[4,128,128]{2,1,0:T(8,128)S(1)}, f32[4,128,128]{2,1,0:T(8,128)}, u32[]{:S(2)}, u32[]{:S(2)}) collective-permute-start(f32[4,128,128]{2,1,0:T(8,128)S(1)} %get-tuple-element.16), channel_id=1, source_target_pairs={{0,1},{1,2},{2,3},{3,4},{4,5},{5,6},{6,7},{7,8},{8,9},{9,10},{10,1... | collective-permute-start | bytes 786440 | tf_op jit(solution)/shard_map/ppermute | solution.py:18
  16.5 7.8 %collective-permute-start.1 = (f32[32,4,128]{2,1,0:T(4,128)S(1)}, f32[32,4,128]{2,1,0:T(4,128)S(1)}, u32[]{:S(2)}, u32[]{:S(2)}) collective-permute-start(f32[32,4,128]{2,1,0:T(4,128)S(1)} %get-tuple-element.29), channel_id=1, source_target_pairs={{16,0},{32,16},{48,32},{64,48},{80,64},{96,80},{112,96},{128,112},... | collective-permute-start | bytes 196616 | tf_op jit(solution)/shard_map/ppermute | solution.py:20
  18.4 6.7 %collective-permute-start = (f32[32,4,128]{2,1,0:T(4,128)S(1)}, f32[32,4,128]{2,1,0:T(4,128)S(1)}, u32[]{:S(2)}, u32[]{:S(2)}) collective-permute-start(f32[32,4,128]{2,1,0:T(4,128)S(1)} %get-tuple-element.28), channel_id=1, source_target_pairs={{0,16},{16,32},{32,48},{48,64},{64,80},{80,96},{96,112},{112,128},... | collective-permute-start | bytes 196616 | tf_op jit(solution)/shard_map/ppermute | solution.py:18
  23.2 19.5 %copy-start = (f32[32,128,128]{2,1,0:T(8,128)S(1)}, f32[32,128,128]{2,1,0:T(8,128)}, u32[]{:S(2)}) copy-start(f32[32,128,128]{2,1,0:T(8,128)} %param.9) | copy-start | bytes 6291460
  25.9 8.1 %collective-permute-start.2 = (f32[4,16,128]{2,1,0:T(8,128)S(1)}, f32[4,16,128]{2,1,0:T(8,128)S(1)}, u32[]{:S(2)}, u32[]{:S(2)}) collective-permute-start(f32[4,16,128]{2,1,0:T(8,128)S(1)} %get-tuple-element.25), channel_id=1, source_target_pairs={{1,0},{2,1},{3,2},{4,3},{5,4},{6,5},{7,6},{8,7},{9,8},{10,9},{11,1... | collective-permute-start | bytes 98312 | tf_op jit(solution)/shard_map/ppermute | solution.py:20
  32.0 8.8 %collective-permute-start.3 = (f32[4,16,128]{2,1,0:T(8,128)S(1)}, f32[4,16,128]{2,1,0:T(8,128)S(1)}, u32[]{:S(2)}, u32[]{:S(2)}) collective-permute-start(f32[4,16,128]{2,1,0:T(8,128)S(1)} %get-tuple-element.24), channel_id=1, source_target_pairs={{0,1},{1,2},{2,3},{3,4},{4,5},{5,6},{6,7},{7,8},{8,9},{9,10},{10,1... | collective-permute-start | bytes 98312 | tf_op jit(solution)/shard_map/ppermute | solution.py:18
  34.0 0.7 copy-start.6
  42.0 0.7 copy-start.8
  58.1 2.2 copy-start.9
  60.3 3.4 %copy-start.1 = (f32[32,128,128]{2,1,0:T(8,128)S(1)}, f32[32,128,128]{2,1,0:T(8,128)}, u32[]{:S(2)}) copy-start(f32[32,128,128]{2,1,0:T(8,128)} %param.9) | copy-start | bytes 6291460
  60.3 3.4 %copy-start.5 = (f32[36,16,128]{2,1,0:T(8,128)S(1)}, f32[36,16,128]{2,1,0:T(8,128)}, u32[]{:S(2)}) copy-start(f32[36,16,128]{2,1,0:T(8,128)} %get-tuple-element.23) | copy-start | bytes 884740
  60.3 3.4 %copy-start.7 = (f32[32,12,128]{2,1,0:T(8,128)S(1)}, f32[32,12,128]{2,1,0:T(8,128)}, u32[]{:S(2)}) copy-start(f32[32,12,128]{2,1,0:T(8,128)} %copy-done.6) | copy-start | bytes 589828
  60.3 3.4 %copy-start.10 = (f32[32,8,128]{2,1,0:T(8,128)S(1)}, f32[32,8,128]{2,1,0:T(8,128)}, u32[]{:S(2)}) copy-start(f32[32,8,128]{2,1,0:T(8,128)} %param.7) | copy-start | bytes 393220
  62.3 1.4 copy-start.2
  66.0 30.6 %copy-start.4 = (f32[32,8,128]{2,1,0:T(8,128)}, f32[32,8,128]{2,1,0:T(8,128)S(1)}, u32[]{:S(2)}) copy-start(f32[32,8,128]{2,1,0:T(8,128)S(1)} %get-tuple-element.6) | copy-start | bytes 393220
  66.0 167.6 %all-gather.5.cloned.1.call-start = ((), (), s32[]{:S(2)}) async-start(), calls=%async_computation.1 | async-start | bytes 2228224 | tf_op jit(solution)/shard_map/all_gather | solution.py:87
  67.1 21.3 %collective-permute-start.10 = (f32[4,128,128]{2,1,0:T(8,128)S(1)}, f32[4,128,128]{2,1,0:T(8,128)S(1)}, u32[]{:S(2)}, u32[]{:S(2)}) collective-permute-start(f32[4,128,128]{2,1,0:T(8,128)S(1)} %get-tuple-element.13), channel_id=1, source_target_pairs={{1,0},{2,1},{3,2},{4,3},{5,4},{6,5},{7,6},{8,7},{9,8},{10,9},{11,1... | collective-permute-start | bytes 786440 | tf_op jit(solution)/shard_map/ppermute | solution.py:20
  69.0 19.4 %collective-permute-start.11 = (f32[4,128,128]{2,1,0:T(8,128)S(1)}, f32[4,128,128]{2,1,0:T(8,128)S(1)}, u32[]{:S(2)}, u32[]{:S(2)}) collective-permute-start(f32[4,128,128]{2,1,0:T(8,128)S(1)} %get-tuple-element.12), channel_id=1, source_target_pairs={{0,1},{1,2},{2,3},{3,4},{4,5},{5,6},{6,7},{7,8},{8,9},{9,10},{10,1... | collective-permute-start | bytes 786440 | tf_op jit(solution)/shard_map/ppermute | solution.py:18
  71.5 7.1 %collective-permute-start.7 = (f32[32,4,128]{2,1,0:T(4,128)S(1)}, f32[32,4,128]{2,1,0:T(4,128)S(1)}, u32[]{:S(2)}, u32[]{:S(2)}) collective-permute-start(f32[32,4,128]{2,1,0:T(4,128)S(1)} %get-tuple-element.27), channel_id=1, source_target_pairs={{16,0},{32,16},{48,32},{64,48},{80,64},{96,80},{112,96},{128,112},... | collective-permute-start | bytes 196616 | tf_op jit(solution)/shard_map/ppermute | solution.py:20
  73.4 7.6 %collective-permute-start.6 = (f32[32,4,128]{2,1,0:T(4,128)S(1)}, f32[32,4,128]{2,1,0:T(4,128)S(1)}, u32[]{:S(2)}, u32[]{:S(2)}) collective-permute-start(f32[32,4,128]{2,1,0:T(4,128)S(1)} %get-tuple-element.26), channel_id=1, source_target_pairs={{0,16},{16,32},{32,48},{48,64},{64,80},{80,96},{96,112},{112,128},... | collective-permute-start | bytes 196616 | tf_op jit(solution)/shard_map/ppermute | solution.py:18
  81.0 13.9 %collective-permute-start.8 = (f32[4,16,128]{2,1,0:T(8,128)S(1)}, f32[4,16,128]{2,1,0:T(8,128)S(1)}, u32[]{:S(2)}, u32[]{:S(2)}) collective-permute-start(f32[4,16,128]{2,1,0:T(8,128)S(1)} %get-tuple-element.21), channel_id=1, source_target_pairs={{1,0},{2,1},{3,2},{4,3},{5,4},{6,5},{7,6},{8,7},{9,8},{10,9},{11,1... | collective-permute-start | bytes 98312 | tf_op jit(solution)/shard_map/ppermute | solution.py:20
  86.3 9.8 %collective-permute-start.9 = (f32[4,16,128]{2,1,0:T(8,128)S(1)}, f32[4,16,128]{2,1,0:T(8,128)S(1)}, u32[]{:S(2)}, u32[]{:S(2)}) collective-permute-start(f32[4,16,128]{2,1,0:T(8,128)S(1)} %get-tuple-element.20), channel_id=1, source_target_pairs={{0,1},{1,2},{2,3},{3,4},{4,5},{5,6},{6,7},{7,8},{8,9},{9,10},{10,1... | collective-permute-start | bytes 98312 | tf_op jit(solution)/shard_map/ppermute | solution.py:18
  201.6 11.1 %collective-permute-start.12 = (f32[4,128,128]{2,1,0:T(8,128)S(1)}, f32[4,128,128]{2,1,0:T(8,128)S(1)}, u32[]{:S(2)}, u32[]{:S(2)}) collective-permute-start(f32[4,128,128]{2,1,0:T(8,128)S(1)} %get-tuple-element.11), channel_id=1, source_target_pairs={{1,0},{2,1},{3,2},{4,3},{5,4},{6,5},{7,6},{8,7},{9,8},{10,9},{11,1... | collective-permute-start | bytes 786440 | tf_op jit(solution)/shard_map/ppermute | solution.py:20
  203.6 14.9 %collective-permute-start.13 = (f32[4,128,128]{2,1,0:T(8,128)S(1)}, f32[4,128,128]{2,1,0:T(8,128)S(1)}, u32[]{:S(2)}, u32[]{:S(2)}) collective-permute-start(f32[4,128,128]{2,1,0:T(8,128)S(1)} %get-tuple-element.10), channel_id=1, source_target_pairs={{0,1},{1,2},{2,3},{3,4},{4,5},{5,6},{6,7},{7,8},{8,9},{9,10},{10,1... | collective-permute-start | bytes 786440 | tf_op jit(solution)/shard_map/ppermute | solution.py:18
Sparse Core Ops, SparseCore 0:
  66.1 86.1 all-gather.2
  154.0 79.5 all-gather.4
where the time goes:
time: 291 us; the launch traced here: 290 us
  other arithmetic  134 us (46%)
  waiting for transfers between devices  85.2 us (29%)
  starting transfers between devices  45 us (15%)
  between operations  14.4 us (5%)
  local copies, waits for them, and re-layouts  11.3 us (4%)
    all_gather x2, waiting for transfers between devices, local(): image_whole = lax.all_gather(image_strip, 'probe', axis=1, tiled=True)  61.9 us
    broadcast_in_dim x1, other arithmetic, local(): born_states[1][None]  49.3 us
    add x1, other arithmetic, local(): 2.0 * newer - older + kappa * born_image + probe_kappa * image_whole  48.3 us
    ppermute x7, starting transfers between devices, extended_2(): lax.ppermute(head, axis, [((i + 1) % count, i) for i in range(ends)])  24.3 us
    ppermute x7, starting transfers between devices, extended_2(): lax.ppermute(tail, axis, [(i, (i + 1) % count) for i in range(ends)])  20.6 us
    concatenate x9, other arithmetic, extended_2(): jnp.concatenate([lax.ppermute(tail, axis, [(i, (i + 1) % count) for i in...  19.9 us
    ppermute x7, waiting for transfers between devices, extended_2(): lax.ppermute(tail, axis, [(i, (i + 1) % count) for i in range(ends)])  16.3 us
    add x2, other arithmetic, derivatives(): gradient = gradient + FIRST[distance] * (higher - deeper)  11.8 us
  transfers between devices with their start and end apart: 16, of which 9 were waited for; matrix products, arithmetic and copies ran while one was open for 24% of the time, Pallas kernels for 0%

commit v1 on v0

--- a/solution.py
+++ b/solution.py
@@ -84,7 +84,9 @@
         extended = jnp.pad(extended, [(0, 0), (0, 0), (4, 4)])
         image_strip = operate(extended, strip_buoyancy, strip_slopes)
         background_next = 2.0 * background_new - background_old + strip_kappa * image_strip
-        image_whole = lax.all_gather(image_strip, "probe", axis=1, tiled=True)
+        image_whole = jnp.concatenate(
+            lax.all_to_all(jnp.stack([image_strip] * lax.axis_size("probe")), "probe", 0, 0), axis=1
+        )
         born_rimmed = extended_2(newer, (("slab", 0),), 4)
         born_image = operate(jnp.pad(born_rimmed, [(0, 0), (4, 4), (4, 4)]), buoyancy, slopes)
         born_next = 2.0 * newer - older + kappa * born_image + probe_kappa * image_whole

time: 291 us -> 261 us (0.90)
  waiting for transfers between devices: 85.2 us -> 48 us
  starting transfers between devices: 45 us -> 63.7 us
  between operations: 14.4 us -> 1.18 us
  local copies, waits for them, and re-layouts: 11.3 us -> 14.4 us
    all_gather x2 -> x0, waiting for transfers between devices: 61.9 us -> none  [local(): image_whole = lax.all_gather(image_strip, 'probe', axis=1, tiled=True)]
    ppermute x7, waiting for transfers between devices: 6.94 us -> 33.4 us  [extended_2(): lax.ppermute(head, axis, [((i + 1) % count, i) for i in range(ends)])]
    all_to_all x0 -> x2, starting transfers between devices: none -> 16.3 us  [local(): lax.all_to_all(jnp.stack([image_strip] * lax.axis_size('probe')), 'probe'...]
    ppermute x7, starting transfers between devices: 24.3 us -> 27.5 us  [extended_2(): lax.ppermute(head, axis, [((i + 1) % count, i) for i in range(ends)])]
    another operation x0 -> x2, local copies, waits for them, and re-layouts: none -> 3.08 us  [local(): jnp.stack([image_strip] * lax.axis_size('probe'))]
  transfers between devices with their start and end apart: 16 -> 16, of which waited for: 9 -> 6; matrix products, arithmetic and copies ran while one was open for 24% -> 27% of each run, Pallas kernels for 0% -> 0%
where the time goes in v1:
time: 261 us; the launch traced here: 260 us
  other arithmetic  132 us (51%)
  starting transfers between devices  63.7 us (24%)
  waiting for transfers between devices  48 us (18%)
  local copies, waits for them, and re-layouts  14.4 us (6%)
    broadcast_in_dim x1, other arithmetic, local(): born_states[1][None]  48.8 us
    add x1, other arithmetic, local(): 2.0 * newer - older + kappa * born_image + probe_kappa * image_whole  47.9 us
    ppermute x7, waiting for transfers between devices, extended_2(): lax.ppermute(head, axis, [((i + 1) % count, i) for i in range(ends)])  33.4 us
    ppermute x7, starting transfers between devices, extended_2(): lax.ppermute(head, axis, [((i + 1) % count, i) for i in range(ends)])  27.5 us
    ppermute x7, starting transfers between devices, extended_2(): lax.ppermute(tail, axis, [(i, (i + 1) % count) for i in range(ends)])  20 us
    concatenate x9, other arithmetic, extended_2(): jnp.concatenate([lax.ppermute(tail, axis, [(i, (i + 1) % count) for i in...  19.9 us
    all_to_all x2, starting transfers between devices, local(): lax.all_to_all(jnp.stack([image_strip] * lax.axis_size('probe')), 'probe'...  16.3 us
    ppermute x7, waiting for transfers between devices, extended_2(): lax.ppermute(tail, axis, [(i, (i + 1) % count) for i in range(ends)])  14.6 us
  transfers between devices with their start and end apart: 16, of which 6 were waited for; matrix products, arithmetic and copies ran while one was open for 27% of the time, Pallas kernels for 0%

profile of v1, /device:TPU:6, one launch (start us, length us, event | category | flops | bytes accessed | tf_op | source)
XLA Modules:
  0.0 259.6 jit_solution(11907586964205626632)
XLA Ops:
  0.6 1.1 fusion.51
  1.8 5.2 %collective-permute-start.4 = (f32[4,128,128]{2,1,0:T(8,128)S(1)}, f32[4,128,128]{2,1,0:T(8,128)S(1)}, u32[]{:S(2)}, u32[]{:S(2)}) collective-permute-start(f32[4,128,128]{2,1,0:T(8,128)S(1)} %get-tuple-element.17), channel_id=1, source_target_pairs={{1,0},{2,1},{3,2},{4,3},{5,4},{6,5},{7,6},{8,7},{9,8},{10,9},{11,1... | collective-permute-start | bytes 786440 | tf_op jit(solution)/shard_map/ppermute | solution.py:20
  7.0 1.9 collective-permute-start.5
  8.9 1.0 fusion.53
  9.9 1.9 collective-permute-start.1
  11.8 4.8 %collective-permute-start = (f32[32,4,128]{2,1,0:T(4,128)S(1)}, f32[32,4,128]{2,1,0:T(4,128)S(1)}, u32[]{:S(2)}, u32[]{:S(2)}) collective-permute-start(f32[32,4,128]{2,1,0:T(4,128)S(1)} %get-tuple-element.28), channel_id=1, source_target_pairs={{0,16},{16,32},{32,48},{48,64},{64,80},{80,96},{96,112},{112,128},... | collective-permute-start | bytes 196616 | tf_op jit(solution)/shard_map/ppermute | solution.py:18
  16.7 1.1 constant_dynamic-update-slice_fusion.1
  17.8 0.8 collective-permute-done
  18.5 0.8 pad_maximum_fusion.12
  19.3 6.1 %collective-permute-start.2 = (f32[4,16,128]{2,1,0:T(8,128)S(1)}, f32[4,16,128]{2,1,0:T(8,128)S(1)}, u32[]{:S(2)}, u32[]{:S(2)}) collective-permute-start(f32[4,16,128]{2,1,0:T(8,128)S(1)} %get-tuple-element.25), channel_id=1, source_target_pairs={{1,0},{2,1},{3,2},{4,3},{5,4},{6,5},{7,6},{8,7},{9,8},{10,9},{11,1... | collective-permute-start | bytes 98312 | tf_op jit(solution)/shard_map/ppermute | solution.py:20
  25.4 1.9 collective-permute-start.3
  27.4 0.7 copy-done.6
  28.1 6.2 %collective-permute-done.3 = f32[4,16,128]{2,1,0:T(8,128)S(1)} collective-permute-done((f32[4,16,128]{2,1,0:T(8,128)S(1)}, f32[4,16,128]{2,1,0:T(8,128)S(1)}, u32[]{:S(2)}, u32[]{:S(2)}) %collective-permute-start.3) | collective-permute-done | bytes 32800 | tf_op jit(solution)/shard_map/ppermute | solution.py:18
  34.3 0.8 pad_maximum_fusion.4
  35.0 0.4 select_maximum_fusion.10
  35.4 0.7 copy-done.8
  36.1 4.6 %select_maximum_fusion.4 = f32[40,136,136]{2,1,0:T(8,128)S(1)} fusion(f32[4,128,128]{2,1,0:T(8,128)} %copy-done.8, f32[32,128,128]{2,1,0:T(8,128)S(1)} %copy-done, f32[4,128,128]{2,1,0:T(8,128)} %collective-permute-done.5), kind=kLoop, calls=%fused_computation.8 | loop fusion | flops 11097600 | bytes 5580800 | tf_op jit(solution)/shard_map/concatenate | solution.py:16
  40.7 9.8 %fusion.23 = (f32[32,128,128]{2,1,0:T(8,128)}, f32[32,128,128]{2,1,0:T(8,128)}) fusion(f32[40,136,136]{2,1,0:T(8,128)S(1)} %select_maximum_fusion.4), kind=kLoop, calls=%fused_computation.66 | loop fusion | flops 11534336 | bytes 37748736 | tf_op jit(solution)/shard_map/add | solution.py:46
  50.5 1.0 constant_dynamic-update-slice_fusion.5
  51.5 2.1 constant_dynamic-update-slice_fusion.3
  53.7 2.0 fusion.30
  55.7 1.4 copy-done.2
  57.1 1.6 multiply_add_fusion.2
  58.8 1.5 stack.4
  60.3 10.7 %all-to-all-start = ((f32[16,32,8,128]{3,2,1,0:T(8,128)}), f32[16,32,8,128]{3,2,1,0:T(8,128)}, u32[]{:S(2)}, u32[]{:S(2)}) async-start(f32[16,32,8,128]{3,2,1,0:T(8,128)} %stack.4), calls=%async_computation | async-start | bytes 4194304 | tf_op jit(solution)/shard_map/all_to_all | solution.py:88
  71.0 1.1 slice_bitcast_fusion
  72.0 1.9 collective-permute-start.10
  74.0 2.4 collective-permute-start.11
  76.4 2.1 collective-permute-start.7
  78.5 4.7 %collective-permute-start.6 = (f32[32,4,128]{2,1,0:T(4,128)S(1)}, f32[32,4,128]{2,1,0:T(4,128)S(1)}, u32[]{:S(2)}, u32[]{:S(2)}) collective-permute-start(f32[32,4,128]{2,1,0:T(4,128)S(1)} %get-tuple-element.26), channel_id=1, source_target_pairs={{0,16},{16,32},{32,48},{48,64},{64,80},{80,96},{96,112},{112,128},... | collective-permute-start | bytes 196616 | tf_op jit(solution)/shard_map/ppermute | solution.py:18
  83.2 31.6 %collective-permute-done.7 = f32[32,4,128]{2,1,0:T(4,128)S(1)} collective-permute-done((f32[32,4,128]{2,1,0:T(4,128)S(1)}, f32[32,4,128]{2,1,0:T(4,128)S(1)}, u32[]{:S(2)}, u32[]{:S(2)}) %collective-permute-start.7) | collective-permute-done | bytes 65568 | tf_op jit(solution)/shard_map/ppermute | solution.py:20
  114.8 3.7 %collective-permute-start.8 = (f32[4,16,128]{2,1,0:T(8,128)S(1)}, f32[4,16,128]{2,1,0:T(8,128)S(1)}, u32[]{:S(2)}, u32[]{:S(2)}) collective-permute-start(f32[4,16,128]{2,1,0:T(8,128)S(1)} %get-tuple-element.21), channel_id=1, source_target_pairs={{1,0},{2,1},{3,2},{4,3},{5,4},{6,5},{7,6},{8,7},{9,8},{10,9},{11,1... | collective-permute-start | bytes 98312 | tf_op jit(solution)/shard_map/ppermute | solution.py:20
  118.5 2.1 collective-permute-start.9
  120.6 6.5 %select_maximum_fusion.2 = f32[40,136,136]{2,1,0:T(8,128)} fusion(f32[4,128,128]{2,1,0:T(8,128)S(1)} %collective-permute-done.10, f32[32,128,128]{2,1,0:T(8,128)} %bitcast.32, f32[4,128,128]{2,1,0:T(8,128)S(1)} %collective-permute-done.11), kind=kLoop, calls=%fused_computation.6 | loop fusion | flops 11097600 | bytes 5580800 | tf_op jit(solution)/shard_map/concatenate | solution.py:16
  127.1 0.2 collective-permute-done.9
  127.4 0.1 pad_maximum_fusion.5
  127.4 0.4 select_maximum_fusion.6
  127.8 2.4 multiply_add_fusion
  130.2 1.6 stack.5
  131.7 5.6 %all-to-all-start.1 = ((f32[16,32,8,128]{3,2,1,0:T(8,128)}), f32[16,32,8,128]{3,2,1,0:T(8,128)}, u32[]{:S(2)}, u32[]{:S(2)}) async-start(f32[16,32,8,128]{3,2,1,0:T(8,128)} %stack.5), calls=%async_computation.1 | async-start | bytes 4194304 | tf_op jit(solution)/shard_map/all_to_all | solution.py:88
  137.3 47.9 %fusion.38 = f32[32,128,128]{2,1,0:T(8,128)} fusion(f32[1,32,128,128]{3,2,1,0:T(8,128)} %param.11, f32[1,32,128,128]{3,2,1,0:T(8,128)} %param.12, f32[16,32,8,128]{3,2,1,0:T(8,128)} %all-to-all-done, f32[32,128,128]{2,1,0:T(8,128)} %param.10, f32[32,128,128]{2,1,0:T(8,128)} %get-tuple-element.9, f32[32,128,128]{2,1,0:T(8,128)} %get-tuple-element.8, ...), kind=kLoop, calls=%fused_computation.90 | loop fusion | flops 47710208 | bytes 55050240 | tf_op jit(solution)/shard_map/add | solution.py:92
  185.2 1.1 fusion.50
  186.3 6.6 %collective-permute-start.12 = (f32[4,128,128]{2,1,0:T(8,128)S(1)}, f32[4,128,128]{2,1,0:T(8,128)S(1)}, u32[]{:S(2)}, u32[]{:S(2)}) collective-permute-start(f32[4,128,128]{2,1,0:T(8,128)S(1)} %get-tuple-element.11), channel_id=1, source_target_pairs={{1,0},{2,1},{3,2},{4,3},{5,4},{6,5},{7,6},{8,7},{9,8},{10,9},{11,1... | collective-permute-start | bytes 786440 | tf_op jit(solution)/shard_map/ppermute | solution.py:20
  192.9 2.1 collective-permute-start.13
  195.0 1.7 collective-permute-done.12
  196.7 7.4 %collective-permute-done.13 = f32[4,128,128]{2,1,0:T(8,128)S(1)} collective-permute-done((f32[4,128,128]{2,1,0:T(8,128)S(1)}, f32[4,128,128]{2,1,0:T(8,128)S(1)}, u32[]{:S(2)}, u32[]{:S(2)}) %collective-permute-start.13) | collective-permute-done | bytes 262176 | tf_op jit(solution)/shard_map/ppermute | solution.py:18
  204.2 6.5 %select_maximum_fusion = f32[40,136,136]{2,1,0:T(8,128)} fusion(f32[4,128,128]{2,1,0:T(8,128)S(1)} %collective-permute-done.12, f32[32,128,128]{2,1,0:T(8,128)} %fusion.38, f32[4,128,128]{2,1,0:T(8,128)S(1)} %collective-permute-done.13), kind=kLoop, calls=%fused_computation.4 | loop fusion | flops 11097600 | bytes 5580800 | tf_op jit(solution)/shard_map/concatenate | solution.py:16
  210.7 48.8 %fusion.37 = f32[1,32,128,128]{3,2,1,0:T(8,128)} fusion(f32[1,32,128,128]{3,2,1,0:T(8,128)} %param.11, f32[16,32,8,128]{3,2,1,0:T(8,128)} %all-to-all-done.1, f32[32,128,128]{2,1,0:T(8,128)} %param.10, f32[32,128,128]{2,1,0:T(8,128)} %get-tuple-element.9, f32[32,128,128]{2,1,0:T(8,128)} %get-tuple-element.8, f32[32,128,128]{2,1,0:T(8,128)} %copy-done.2, ...), kind=kLoop, calls=%fused_computation.88 | loop fusion | flops 47710208 | bytes 55050240 | tf_op jit(solution)/shard_map/broadcast_in_dim | solution.py:97
  (33 shorter events, 0.2 us)
Async XLA Ops:
  0.6 33.6 %copy-start.3 = (f32[32,8,128]{2,1,0:T(8,128)S(1)}, f32[32,8,128]{2,1,0:T(8,128)}, u32[]{:S(2)}) copy-start(f32[32,8,128]{2,1,0:T(8,128)} %param.8) | copy-start | bytes 393220
  1.8 33.7 %collective-permute-start.4 = (f32[4,128,128]{2,1,0:T(8,128)S(1)}, f32[4,128,128]{2,1,0:T(8,128)S(1)}, u32[]{:S(2)}, u32[]{:S(2)}) collective-permute-start(f32[4,128,128]{2,1,0:T(8,128)S(1)} %get-tuple-element.17), channel_id=1, source_target_pairs={{1,0},{2,1},{3,2},{4,3},{5,4},{6,5},{7,6},{8,7},{9,8},{10,9},{11,1... | collective-permute-start | bytes 786440 | tf_op jit(solution)/shard_map/ppermute | solution.py:20
  7.0 29.2 %collective-permute-start.5 = (f32[4,128,128]{2,1,0:T(8,128)S(1)}, f32[4,128,128]{2,1,0:T(8,128)}, u32[]{:S(2)}, u32[]{:S(2)}) collective-permute-start(f32[4,128,128]{2,1,0:T(8,128)S(1)} %get-tuple-element.16), channel_id=1, source_target_pairs={{0,1},{1,2},{2,3},{3,4},{4,5},{5,6},{6,7},{7,8},{8,9},{9,10},{10,1... | collective-permute-start | bytes 786440 | tf_op jit(solution)/shard_map/ppermute | solution.py:18
  9.9 7.8 %collective-permute-start.1 = (f32[32,4,128]{2,1,0:T(4,128)S(1)}, f32[32,4,128]{2,1,0:T(4,128)S(1)}, u32[]{:S(2)}, u32[]{:S(2)}) collective-permute-start(f32[32,4,128]{2,1,0:T(4,128)S(1)} %get-tuple-element.29), channel_id=1, source_target_pairs={{16,0},{32,16},{48,32},{64,48},{80,64},{96,80},{112,96},{128,112},... | collective-permute-start | bytes 196616 | tf_op jit(solution)/shard_map/ppermute | solution.py:20
  11.8 6.7 %collective-permute-start = (f32[32,4,128]{2,1,0:T(4,128)S(1)}, f32[32,4,128]{2,1,0:T(4,128)S(1)}, u32[]{:S(2)}, u32[]{:S(2)}) collective-permute-start(f32[32,4,128]{2,1,0:T(4,128)S(1)} %get-tuple-element.28), channel_id=1, source_target_pairs={{0,16},{16,32},{32,48},{48,64},{64,80},{80,96},{96,112},{112,128},... | collective-permute-start | bytes 196616 | tf_op jit(solution)/shard_map/ppermute | solution.py:18
  16.7 19.5 %copy-start = (f32[32,128,128]{2,1,0:T(8,128)S(1)}, f32[32,128,128]{2,1,0:T(8,128)}, u32[]{:S(2)}) copy-start(f32[32,128,128]{2,1,0:T(8,128)} %param.9) | copy-start | bytes 6291460
  19.3 8.1 %collective-permute-start.2 = (f32[4,16,128]{2,1,0:T(8,128)S(1)}, f32[4,16,128]{2,1,0:T(8,128)S(1)}, u32[]{:S(2)}, u32[]{:S(2)}) collective-permute-start(f32[4,16,128]{2,1,0:T(8,128)S(1)} %get-tuple-element.25), channel_id=1, source_target_pairs={{1,0},{2,1},{3,2},{4,3},{5,4},{6,5},{7,6},{8,7},{9,8},{10,9},{11,1... | collective-permute-start | bytes 98312 | tf_op jit(solution)/shard_map/ppermute | solution.py:20
  25.4 8.8 %collective-permute-start.3 = (f32[4,16,128]{2,1,0:T(8,128)S(1)}, f32[4,16,128]{2,1,0:T(8,128)S(1)}, u32[]{:S(2)}, u32[]{:S(2)}) collective-permute-start(f32[4,16,128]{2,1,0:T(8,128)S(1)} %get-tuple-element.24), channel_id=1, source_target_pairs={{0,1},{1,2},{2,3},{3,4},{4,5},{5,6},{6,7},{7,8},{8,9},{9,10},{10,1... | collective-permute-start | bytes 98312 | tf_op jit(solution)/shard_map/ppermute | solution.py:18
  27.4 0.7 copy-start.6
  35.4 0.7 copy-start.8
  51.5 2.2 copy-start.9
  53.7 3.4 %copy-start.1 = (f32[32,128,128]{2,1,0:T(8,128)S(1)}, f32[32,128,128]{2,1,0:T(8,128)}, u32[]{:S(2)}) copy-start(f32[32,128,128]{2,1,0:T(8,128)} %param.9) | copy-start | bytes 6291460
  53.7 3.4 %copy-start.5 = (f32[36,16,128]{2,1,0:T(8,128)S(1)}, f32[36,16,128]{2,1,0:T(8,128)}, u32[]{:S(2)}) copy-start(f32[36,16,128]{2,1,0:T(8,128)} %get-tuple-element.23) | copy-start | bytes 884740
  53.7 3.4 %copy-start.7 = (f32[32,12,128]{2,1,0:T(8,128)S(1)}, f32[32,12,128]{2,1,0:T(8,128)}, u32[]{:S(2)}) copy-start(f32[32,12,128]{2,1,0:T(8,128)} %copy-done.6) | copy-start | bytes 589828
  53.7 3.4 %copy-start.10 = (f32[32,8,128]{2,1,0:T(8,128)S(1)}, f32[32,8,128]{2,1,0:T(8,128)}, u32[]{:S(2)}) copy-start(f32[32,8,128]{2,1,0:T(8,128)} %param.7) | copy-start | bytes 393220
  55.7 1.4 copy-start.2
  58.7 69.0 %copy-start.4 = (f32[32,8,128]{2,1,0:T(8,128)}, f32[32,8,128]{2,1,0:T(8,128)S(1)}, u32[]{:S(2)}) copy-start(f32[32,8,128]{2,1,0:T(8,128)S(1)} %get-tuple-element.6) | copy-start | bytes 393220
  60.3 69.9 %all-to-all-start = ((f32[16,32,8,128]{3,2,1,0:T(8,128)}), f32[16,32,8,128]{3,2,1,0:T(8,128)}, u32[]{:S(2)}, u32[]{:S(2)}) async-start(f32[16,32,8,128]{3,2,1,0:T(8,128)} %stack.4), calls=%async_computation | async-start | bytes 4194304 | tf_op jit(solution)/shard_map/all_to_all | solution.py:88
  72.0 48.6 %collective-permute-start.10 = (f32[4,128,128]{2,1,0:T(8,128)S(1)}, f32[4,128,128]{2,1,0:T(8,128)S(1)}, u32[]{:S(2)}, u32[]{:S(2)}) collective-permute-start(f32[4,128,128]{2,1,0:T(8,128)S(1)} %get-tuple-element.13), channel_id=1, source_target_pairs={{1,0},{2,1},{3,2},{4,3},{5,4},{6,5},{7,6},{8,7},{9,8},{10,9},{11,1... | collective-permute-start | bytes 786440 | tf_op jit(solution)/shard_map/ppermute | solution.py:20
  74.0 46.7 %collective-permute-start.11 = (f32[4,128,128]{2,1,0:T(8,128)S(1)}, f32[4,128,128]{2,1,0:T(8,128)S(1)}, u32[]{:S(2)}, u32[]{:S(2)}) collective-permute-start(f32[4,128,128]{2,1,0:T(8,128)S(1)} %get-tuple-element.12), channel_id=1, source_target_pairs={{0,1},{1,2},{2,3},{3,4},{4,5},{5,6},{6,7},{7,8},{8,9},{9,10},{10,1... | collective-permute-start | bytes 786440 | tf_op jit(solution)/shard_map/ppermute | solution.py:18
  76.4 38.4 %collective-permute-start.7 = (f32[32,4,128]{2,1,0:T(4,128)S(1)}, f32[32,4,128]{2,1,0:T(4,128)S(1)}, u32[]{:S(2)}, u32[]{:S(2)}) collective-permute-start(f32[32,4,128]{2,1,0:T(4,128)S(1)} %get-tuple-element.27), channel_id=1, source_target_pairs={{16,0},{32,16},{48,32},{64,48},{80,64},{96,80},{112,96},{128,112},... | collective-permute-start | bytes 196616 | tf_op jit(solution)/shard_map/ppermute | solution.py:20
  78.5 36.3 %collective-permute-start.6 = (f32[32,4,128]{2,1,0:T(4,128)S(1)}, f32[32,4,128]{2,1,0:T(4,128)S(1)}, u32[]{:S(2)}, u32[]{:S(2)}) collective-permute-start(f32[32,4,128]{2,1,0:T(4,128)S(1)} %get-tuple-element.26), channel_id=1, source_target_pairs={{0,16},{16,32},{32,48},{48,64},{64,80},{80,96},{96,112},{112,128},... | collective-permute-start | bytes 196616 | tf_op jit(solution)/shard_map/ppermute | solution.py:18
  114.8 12.3 %collective-permute-start.8 = (f32[4,16,128]{2,1,0:T(8,128)S(1)}, f32[4,16,128]{2,1,0:T(8,128)S(1)}, u32[]{:S(2)}, u32[]{:S(2)}) collective-permute-start(f32[4,16,128]{2,1,0:T(8,128)S(1)} %get-tuple-element.21), channel_id=1, source_target_pairs={{1,0},{2,1},{3,2},{4,3},{5,4},{6,5},{7,6},{8,7},{9,8},{10,9},{11,1... | collective-permute-start | bytes 98312 | tf_op jit(solution)/shard_map/ppermute | solution.py:20
  118.5 8.8 %collective-permute-start.9 = (f32[4,16,128]{2,1,0:T(8,128)S(1)}, f32[4,16,128]{2,1,0:T(8,128)S(1)}, u32[]{:S(2)}, u32[]{:S(2)}) collective-permute-start(f32[4,16,128]{2,1,0:T(8,128)S(1)} %get-tuple-element.20), channel_id=1, source_target_pairs={{0,1},{1,2},{2,3},{3,4},{4,5},{5,6},{6,7},{7,8},{8,9},{9,10},{10,1... | collective-permute-start | bytes 98312 | tf_op jit(solution)/shard_map/ppermute | solution.py:18
  131.7 78.9 %all-to-all-start.1 = ((f32[16,32,8,128]{3,2,1,0:T(8,128)}), f32[16,32,8,128]{3,2,1,0:T(8,128)}, u32[]{:S(2)}, u32[]{:S(2)}) async-start(f32[16,32,8,128]{3,2,1,0:T(8,128)} %stack.5), calls=%async_computation.1 | async-start | bytes 4194304 | tf_op jit(solution)/shard_map/all_to_all | solution.py:88
  186.3 10.4 %collective-permute-start.12 = (f32[4,128,128]{2,1,0:T(8,128)S(1)}, f32[4,128,128]{2,1,0:T(8,128)S(1)}, u32[]{:S(2)}, u32[]{:S(2)}) collective-permute-start(f32[4,128,128]{2,1,0:T(8,128)S(1)} %get-tuple-element.11), channel_id=1, source_target_pairs={{1,0},{2,1},{3,2},{4,3},{5,4},{6,5},{7,6},{8,7},{9,8},{10,9},{11,1... | collective-permute-start | bytes 786440 | tf_op jit(solution)/shard_map/ppermute | solution.py:20
  192.9 11.3 %collective-permute-start.13 = (f32[4,128,128]{2,1,0:T(8,128)S(1)}, f32[4,128,128]{2,1,0:T(8,128)S(1)}, u32[]{:S(2)}, u32[]{:S(2)}) collective-permute-start(f32[4,128,128]{2,1,0:T(8,128)S(1)} %get-tuple-element.10), channel_id=1, source_target_pairs={{0,1},{1,2},{2,3},{3,4},{4,5},{5,6},{6,7},{7,8},{8,9},{9,10},{10,1... | collective-permute-start | bytes 786440 | tf_op jit(solution)/shard_map/ppermute | solution.py:18
